TPU v7x, 32 devices: a whole 2x2x4 slice. The times are simulated.
32 devices in a mesh: tensor: 4 (over x, core), replica: 4 (over z), fsdp: 2 (over y).
Axes of the slice: x: 2, y: 2, z: 4, core: 2. Of those that a mesh axis runs over, the one named last changes fastest.
Arguments:
- gradients: bfloat16 [4, 128, 28672], P('replica', 'fsdp', 'tensor'), may hold values from -6 to 6
- seeds: int32 [2], replicated, may hold values from 0 to 1073741823
- adam_step: int32 [1], replicated, may hold values from 1 to 8
- first_moment: float32 [128, 28672], P(('fsdp', 'replica'), 'tensor'), may hold values from -0.6 to 0.6
- second_moment: float32 [128, 28672], P(('fsdp', 'replica'), 'tensor'), may hold values from 0.001 to 0.1
Outputs:
- new_first: float32 [128, 28672], P(('fsdp', 'replica'), 'tensor')
- new_second: float32 [128, 28672], P(('fsdp', 'replica'), 'tensor')
- step_update: float32 [128, 28672], P(('fsdp', 'replica'), 'tensor')
All inputs are finite; a program needn't handle non-finite values.
Results may differ from a plain program's by a relative error of at most 0.012.
The roundings to bfloat16 on the way count: a program that leaves them out, or rounds other values in their place, can miss the bound.
Values may be sent and summed in bfloat16 or wider, within the bound.
No kernel may reach another device: no remote copies, remote signals or barrier semaphores. Data moves between devices by JAX's collectives and lax.ppermute only.
A program may use at most 64 MiB of HBM per device.

v0:
```python
import math
import jax
import jax.numpy as jnp
from jax import lax
from jax.sharding import PartitionSpec as P

RANK = 512


def scramble(value):
    value = value ^ lax.shift_right_logical(value, jnp.full_like(value, 16))
    value = value * jnp.int32(-2048144789)
    value = value ^ lax.shift_right_logical(value, jnp.full_like(value, 13))
    value = value * jnp.int32(-1028477387)
    value = value ^ lax.shift_right_logical(value, jnp.full_like(value, 16))
    return value


def projection_block(first_column, columns, rank, seeds):
    seed_key = seeds[0] ^ seeds[1] * jnp.int32(668265263)
    column = lax.broadcasted_iota(jnp.int32, (columns, rank), 0) + first_column
    entry = lax.broadcasted_iota(jnp.int32, (columns, rank), 1)
    counter = (column * jnp.int32(rank) + entry) * jnp.int32(2)
    hash_a = scramble(counter * jnp.int32(-1640531535) ^ seed_key)
    hash_b = scramble((counter + jnp.int32(1)) * jnp.int32(-1640531535) ^ seed_key)
    inverse = 1.0 / 16777216.0
    uniform_a = (
        lax.shift_right_logical(hash_a, jnp.full_like(hash_a, 8)).astype(jnp.float32) + 0.5
    ) * inverse
    uniform_b = (
        lax.shift_right_logical(hash_b, jnp.full_like(hash_b, 8)).astype(jnp.float32) + 0.5
    ) * inverse
    gauss = jnp.sqrt(-2.0 * jnp.log(uniform_a)) * jnp.cos(6.283185307179586 * uniform_b)
    return (gauss * rank ** (-0.5)).astype(jnp.bfloat16)


def per_device(gradients, seeds, adam_step, first_moment, second_moment):
    gradient = gradients[0]
    columns = gradient.shape[1]
    replicas = lax.axis_size("replica")
    column_start = lax.axis_index("tensor") * jnp.int32(columns)
    piece_cols = math.gcd(columns, 512)
    blocks = columns // piece_cols
    starts = column_start + lax.iota(jnp.int32, blocks) * jnp.int32(piece_cols)
    tiles = lax.map(lambda first: projection_block(first, piece_cols, RANK, seeds), starts)
    projection = tiles.reshape(columns, RANK)
    partial_value = jnp.dot(gradient, projection, preferred_element_type=jnp.float32) * (
        1.0 / replicas
    )
    share = lax.psum_scatter(partial_value, "replica", scatter_dimension=0, tiled=True)
    sketch = lax.psum(share, "tensor")
    sketch_rounded = sketch.astype(jnp.bfloat16)
    estimate = lax.dot_general(
        sketch_rounded, projection, (((1,), (1,)), ((), ())), preferred_element_type=jnp.float32
    )
    new_first = 0.9 * first_moment + 0.1 * estimate
    new_second = 0.95 * second_moment + 0.05 * estimate * estimate
    step_float = adam_step[0].astype(jnp.float32)
    fix_first = 1.0 - jnp.power(jnp.float32(0.9), step_float)
    fix_second = 1.0 - jnp.power(jnp.float32(0.95), step_float)
    step_update = new_first / fix_first / (jnp.sqrt(new_second / fix_second) + 1e-08)
    return (new_first, new_second, step_update)


def solution(mesh):
    placed = (
        P("replica", "fsdp", "tensor"),
        P(),
        P(),
        P(("fsdp", "replica"), "tensor"),
        P(("fsdp", "replica"), "tensor"),
    )
    return jax.shard_map(
        per_device,
        mesh=mesh,
        in_specs=placed,
        out_specs=(
            P(("fsdp", "replica"), "tensor"),
            P(("fsdp", "replica"), "tensor"),
            P(("fsdp", "replica"), "tensor"),
        ),
        check_vma=False,
    )
```

profile of v0, /device:TPU:1, one launch (start us, length us, event | category | flops | bytes accessed | tf_op | source)
XLA Modules:
  0.0 164.6 jit_solution(9987295474891056560)
XLA Ops:
  7.2 1.3 fusion.26
  9.9 99.4 %while.12 = (s32[]{:T(128)}, bf16[14,512,512]{2,1,0:T(8,128)(2,1)}, s32[14]{0:T(128)S(1)}, s32[]{:T(128)}, s32[]{:T(128)}) while((s32[]{:T(128)}, bf16[14,512,512]{2,1,0:T(8,128)(2,1)}, s32[14]{0:T(128)S(1)}, s32[]{:T(128)}, s32[]{:T(128)}) %tuple.33), condition=%wide.region_1.2_spmd, body=%wide.region_0.1_spmd.sunk | while | flops 9176066 | bytes 529485 | solution.py:45
  9.9 0.6 dynamic_slice.8
  10.5 0.6 add_multiply_fusion.2
  11.1 5.9 %fusion.31 = bf16[14,512,512]{2,1,0:T(8,128)(2,1)} fusion(bf16[14,512,512]{2,1,0:T(8,128)(2,1)} %get-tuple-element.105, s32[]{:T(128)} %get-tuple-element.104, s32[]{:T(128)} %get-tuple-element.112, s32[512]{0:T(512)S(1)} %add_multiply_fusion.2), kind=kLoop, calls=%fused_computation.25.clone.1 | loop fusion | flops 9175040 | bytes 527360 | tf_op jit(solution)/shard_map/while/body/jit(dynamic_update_index_in_dim)/dynamic_update_slice | solution.py:45
  17.0 0.6 dynamic_slice.8
  17.6 0.6 add_multiply_fusion.2
  18.2 5.9 %fusion.31 = bf16[14,512,512]{2,1,0:T(8,128)(2,1)} fusion(bf16[14,512,512]{2,1,0:T(8,128)(2,1)} %get-tuple-element.105, s32[]{:T(128)} %get-tuple-element.104, s32[]{:T(128)} %get-tuple-element.112, s32[512]{0:T(512)S(1)} %add_multiply_fusion.2), kind=kLoop, calls=%fused_computation.25.clone.1 | loop fusion | flops 9175040 | bytes 527360 | tf_op jit(solution)/shard_map/while/body/jit(dynamic_update_index_in_dim)/dynamic_update_slice | solution.py:45
  24.1 0.6 dynamic_slice.8
  24.7 0.6 add_multiply_fusion.2
  25.3 5.9 %fusion.31 = bf16[14,512,512]{2,1,0:T(8,128)(2,1)} fusion(bf16[14,512,512]{2,1,0:T(8,128)(2,1)} %get-tuple-element.105, s32[]{:T(128)} %get-tuple-element.104, s32[]{:T(128)} %get-tuple-element.112, s32[512]{0:T(512)S(1)} %add_multiply_fusion.2), kind=kLoop, calls=%fused_computation.25.clone.1 | loop fusion | flops 9175040 | bytes 527360 | tf_op jit(solution)/shard_map/while/body/jit(dynamic_update_index_in_dim)/dynamic_update_slice | solution.py:45
  31.2 0.6 dynamic_slice.8
  31.8 0.6 add_multiply_fusion.2
  32.4 5.9 %fusion.31 = bf16[14,512,512]{2,1,0:T(8,128)(2,1)} fusion(bf16[14,512,512]{2,1,0:T(8,128)(2,1)} %get-tuple-element.105, s32[]{:T(128)} %get-tuple-element.104, s32[]{:T(128)} %get-tuple-element.112, s32[512]{0:T(512)S(1)} %add_multiply_fusion.2), kind=kLoop, calls=%fused_computation.25.clone.1 | loop fusion | flops 9175040 | bytes 527360 | tf_op jit(solution)/shard_map/while/body/jit(dynamic_update_index_in_dim)/dynamic_update_slice | solution.py:45
  38.3 0.6 dynamic_slice.8
  38.9 0.6 add_multiply_fusion.2
  39.5 5.8 %fusion.31 = bf16[14,512,512]{2,1,0:T(8,128)(2,1)} fusion(bf16[14,512,512]{2,1,0:T(8,128)(2,1)} %get-tuple-element.105, s32[]{:T(128)} %get-tuple-element.104, s32[]{:T(128)} %get-tuple-element.112, s32[512]{0:T(512)S(1)} %add_multiply_fusion.2), kind=kLoop, calls=%fused_computation.25.clone.1 | loop fusion | flops 9175040 | bytes 527360 | tf_op jit(solution)/shard_map/while/body/jit(dynamic_update_index_in_dim)/dynamic_update_slice | solution.py:45
  45.4 0.6 dynamic_slice.8
  46.0 0.6 add_multiply_fusion.2
  46.6 5.9 %fusion.31 = bf16[14,512,512]{2,1,0:T(8,128)(2,1)} fusion(bf16[14,512,512]{2,1,0:T(8,128)(2,1)} %get-tuple-element.105, s32[]{:T(128)} %get-tuple-element.104, s32[]{:T(128)} %get-tuple-element.112, s32[512]{0:T(512)S(1)} %add_multiply_fusion.2), kind=kLoop, calls=%fused_computation.25.clone.1 | loop fusion | flops 9175040 | bytes 527360 | tf_op jit(solution)/shard_map/while/body/jit(dynamic_update_index_in_dim)/dynamic_update_slice | solution.py:45
  52.5 0.6 dynamic_slice.8
  53.0 0.6 add_multiply_fusion.2
  53.7 5.9 %fusion.31 = bf16[14,512,512]{2,1,0:T(8,128)(2,1)} fusion(bf16[14,512,512]{2,1,0:T(8,128)(2,1)} %get-tuple-element.105, s32[]{:T(128)} %get-tuple-element.104, s32[]{:T(128)} %get-tuple-element.112, s32[512]{0:T(512)S(1)} %add_multiply_fusion.2), kind=kLoop, calls=%fused_computation.25.clone.1 | loop fusion | flops 9175040 | bytes 527360 | tf_op jit(solution)/shard_map/while/body/jit(dynamic_update_index_in_dim)/dynamic_update_slice | solution.py:45
  59.6 0.6 dynamic_slice.8
  60.1 0.6 add_multiply_fusion.2
  60.8 5.9 %fusion.31 = bf16[14,512,512]{2,1,0:T(8,128)(2,1)} fusion(bf16[14,512,512]{2,1,0:T(8,128)(2,1)} %get-tuple-element.105, s32[]{:T(128)} %get-tuple-element.104, s32[]{:T(128)} %get-tuple-element.112, s32[512]{0:T(512)S(1)} %add_multiply_fusion.2), kind=kLoop, calls=%fused_computation.25.clone.1 | loop fusion | flops 9175040 | bytes 527360 | tf_op jit(solution)/shard_map/while/body/jit(dynamic_update_index_in_dim)/dynamic_update_slice | solution.py:45
  66.7 0.6 dynamic_slice.8
  67.2 0.6 add_multiply_fusion.2
  67.9 5.9 %fusion.31 = bf16[14,512,512]{2,1,0:T(8,128)(2,1)} fusion(bf16[14,512,512]{2,1,0:T(8,128)(2,1)} %get-tuple-element.105, s32[]{:T(128)} %get-tuple-element.104, s32[]{:T(128)} %get-tuple-element.112, s32[512]{0:T(512)S(1)} %add_multiply_fusion.2), kind=kLoop, calls=%fused_computation.25.clone.1 | loop fusion | flops 9175040 | bytes 527360 | tf_op jit(solution)/shard_map/while/body/jit(dynamic_update_index_in_dim)/dynamic_update_slice | solution.py:45
  73.8 0.6 dynamic_slice.8
  74.3 0.6 add_multiply_fusion.2
  75.0 5.9 %fusion.31 = bf16[14,512,512]{2,1,0:T(8,128)(2,1)} fusion(bf16[14,512,512]{2,1,0:T(8,128)(2,1)} %get-tuple-element.105, s32[]{:T(128)} %get-tuple-element.104, s32[]{:T(128)} %get-tuple-element.112, s32[512]{0:T(512)S(1)} %add_multiply_fusion.2), kind=kLoop, calls=%fused_computation.25.clone.1 | loop fusion | flops 9175040 | bytes 527360 | tf_op jit(solution)/shard_map/while/body/jit(dynamic_update_index_in_dim)/dynamic_update_slice | solution.py:45
  80.9 0.6 dynamic_slice.8
  81.4 0.6 add_multiply_fusion.2
  82.1 5.9 %fusion.31 = bf16[14,512,512]{2,1,0:T(8,128)(2,1)} fusion(bf16[14,512,512]{2,1,0:T(8,128)(2,1)} %get-tuple-element.105, s32[]{:T(128)} %get-tuple-element.104, s32[]{:T(128)} %get-tuple-element.112, s32[512]{0:T(512)S(1)} %add_multiply_fusion.2), kind=kLoop, calls=%fused_computation.25.clone.1 | loop fusion | flops 9175040 | bytes 527360 | tf_op jit(solution)/shard_map/while/body/jit(dynamic_update_index_in_dim)/dynamic_update_slice | solution.py:45
  88.5 0.6 add_multiply_fusion.2
  89.2 5.9 %fusion.31 = bf16[14,512,512]{2,1,0:T(8,128)(2,1)} fusion(bf16[14,512,512]{2,1,0:T(8,128)(2,1)} %get-tuple-element.105, s32[]{:T(128)} %get-tuple-element.104, s32[]{:T(128)} %get-tuple-element.112, s32[512]{0:T(512)S(1)} %add_multiply_fusion.2), kind=kLoop, calls=%fused_computation.25.clone.1 | loop fusion | flops 9175040 | bytes 527360 | tf_op jit(solution)/shard_map/while/body/jit(dynamic_update_index_in_dim)/dynamic_update_slice | solution.py:45
  95.1 0.6 dynamic_slice.8
  95.6 0.6 add_multiply_fusion.2
  96.3 5.9 %fusion.31 = bf16[14,512,512]{2,1,0:T(8,128)(2,1)} fusion(bf16[14,512,512]{2,1,0:T(8,128)(2,1)} %get-tuple-element.105, s32[]{:T(128)} %get-tuple-element.104, s32[]{:T(128)} %get-tuple-element.112, s32[512]{0:T(512)S(1)} %add_multiply_fusion.2), kind=kLoop, calls=%fused_computation.25.clone.1 | loop fusion | flops 9175040 | bytes 527360 | tf_op jit(solution)/shard_map/while/body/jit(dynamic_update_index_in_dim)/dynamic_update_slice | solution.py:45
  102.7 0.6 add_multiply_fusion.2
  103.4 5.9 %fusion.31 = bf16[14,512,512]{2,1,0:T(8,128)(2,1)} fusion(bf16[14,512,512]{2,1,0:T(8,128)(2,1)} %get-tuple-element.105, s32[]{:T(128)} %get-tuple-element.104, s32[]{:T(128)} %get-tuple-element.112, s32[512]{0:T(512)S(1)} %add_multiply_fusion.2), kind=kLoop, calls=%fused_computation.25.clone.1 | loop fusion | flops 9175040 | bytes 527360 | tf_op jit(solution)/shard_map/while/body/jit(dynamic_update_index_in_dim)/dynamic_update_slice | solution.py:45
  109.2 5.2 %fusion.20 = f32[64,512]{0,1:T(8,128)S(1)} fusion(bf16[7168,512]{1,0:T(8,128)(2,1)} %bitcast.16, bf16[1,64,7168]{2,1,0:T(8,128)(2,1)S(1)} %copy-done), kind=kOutput, calls=%fused_computation.28 | convolution fusion | flops 469794816 | bytes 8388608 | tf_op jit(solution)/shard_map/dot_general | solution.py:47
  114.4 0.8 copy.8
  116.0 18.6 %reduce-scatter.4.cloned.1.call-done = f32[16,512]{1,0:T(8,128)} async-done(((f32[64,512]{1,0:T(8,128)}), f32[16,512]{1,0:T(8,128)}) %reduce-scatter.4.cloned.1.call-update) | async-done | bytes 32784
  134.5 0.9 copy.9
  135.4 16.2 %psum.7 = bf16[16,512]{0,1:T(8,128)(2,1)S(1)} all-reduce(f32[16,512]{0,1:T(8,128)S(1)} %copy.9), channel_id=1, replica_groups=mesh['tensor'=4,'replica'=4,'fsdp'=2] {'tensor'}, use_global_device_ids=true, to_apply=%region_3.4 | all-reduce | flops 8192 | bytes 49152 | tf_op jit(solution)/shard_map/psum | solution.py:51
  151.6 6.2 %multiply_divide_fusion = (f32[16,7168]{1,0:T(8,128)}, f32[16,7168]{1,0:T(8,128)}, f32[16,7168]{1,0:T(8,128)}) fusion(f32[]{:T(128)} %bitcast.6, f32[]{:T(128)} %bitcast.5, f32[16,7168]{1,0:T(8,128)S(1)} %copy-done.1, f32[16,7168]{1,0:T(8,128)S(1)} %copy-done.2, bf16[16,512]{0,1:T(8,128)(2,1)S(1)} %psum.7, bf16[7168,512]{1,0:T(8,128)(2,1)} %bitcast.17), kind=kOutput, calls=%fused_computation.32 | convolution fusion | flops 118702080 | bytes 9650184 | tf_op jit(solution)/shard_map/dot_general | solution.py:53
  (12 shorter events, 1.2 us)
Async XLA Ops:
  7.2 102.1 %copy-start = (bf16[1,64,7168]{2,1,0:T(8,128)(2,1)S(1)}, bf16[1,64,7168]{2,1,0:T(8,128)(2,1)}, u32[]{:S(2)}) copy-start(bf16[1,64,7168]{2,1,0:T(8,128)(2,1)} %param.7) | copy-start | bytes 2752516
  7.2 127.3 %reduce-scatter.4.cloned.1.call-start = ((), (), s32[]{:S(2)}) async-start(), calls=%async_computation.1 | async-start | bytes 163840
  9.9 141.7 %copy-start.1 = (f32[16,7168]{1,0:T(8,128)S(1)}, f32[16,7168]{1,0:T(8,128)}, u32[]{:S(2)}) copy-start(f32[16,7168]{1,0:T(8,128)} %param.11) | copy-start | bytes 1376260
  9.9 141.7 %copy-start.2 = (f32[16,7168]{1,0:T(8,128)S(1)}, f32[16,7168]{1,0:T(8,128)}, u32[]{:S(2)}) copy-start(f32[16,7168]{1,0:T(8,128)} %param.10) | copy-start | bytes 1376260
Sparse Core Ops, SparseCore 0:
  115.3 19.1 reduce-scatter.3
where the time goes:
time: 165 us
  other arithmetic  91.1 us (55%)
  waiting for transfers between devices  18.6 us (11%)
  blocking collectives  16.2 us (10%)
  between operations  16.1 us (10%)
  matrix products  11.4 us (7%)
  local copies, waits for them, and re-layouts  11.2 us (7%)
    dynamic_update_slice x14, other arithmetic, per_device(): lax.map(lambda first: projection_block(first, piece_cols, RANK, seeds), s...  82 us
    unnamed x2, waiting for transfers between devices  18.6 us
    psum x1, blocking collectives, per_device(): sketch = lax.psum(share, 'tensor')  16.2 us
    mul x14, other arithmetic, projection_block(): counter = (column * jnp.int32(rank) + entry) * jnp.int32(2)  9.07 us
    dynamic_slice x14, local copies, waits for them, and re-layouts, per_device(): lax.map(lambda first: projection_block(first, piece_cols, RANK, seeds), s...  8.15 us
    dot_general x1, matrix products, per_device(): lax.dot_general(sketch_rounded, projection, (((1,), (1,)), ((), ())), pre...  6.19 us
    dot_general x1, matrix products, per_device(): jnp.dot(gradient, projection, preferred_element_type=jnp.float32)  5.17 us
  transfers between devices with their start and end apart: 1, of which 1 were waited for; matrix products, arithmetic and copies ran while one was open for 0% of the time, Pallas kernels for 0%

commit v1 on v0

--- a/solution.py
+++ b/solution.py
@@ -48,7 +48,9 @@
         1.0 / replicas
     )
     share = lax.psum_scatter(partial_value, "replica", scatter_dimension=0, tiled=True)
-    sketch = lax.psum(share, "tensor")
+    sketch = share
+    for hop in (1, 2):
+        sketch = sketch + lax.ppermute(sketch, "tensor", [(dev, dev ^ hop) for dev in range(4)])
     sketch_rounded = sketch.astype(jnp.bfloat16)
     estimate = lax.dot_general(
         sketch_rounded, projection, (((1,), (1,)), ((), ())), preferred_element_type=jnp.float32

time: 165 us -> 156 us (0.945)
  blocking collectives: 16.2 us -> 0 us
  starting transfers between devices: 0.04 us -> 4.25 us
  waiting for transfers between devices: 18.6 us -> 21.2 us
  local copies, waits for them, and re-layouts: 11.2 us -> 9.49 us
    reduce_scatter x0 -> x1, waiting for transfers between devices: none -> 19.3 us  [per_device(): lax.psum_scatter(partial_value, 'replica', scatter_dimension=0, tiled=True)]
    unnamed x2 -> x1, waiting for transfers between devices: 18.6 us -> 0.02 us
    psum x1 -> x0, blocking collectives: 16.2 us -> none  [per_device(): sketch = lax.psum(share, 'tensor')]
    ppermute x0 -> x2, starting transfers between devices: none -> 4.22 us  [per_device(): lax.ppermute(sketch, 'tensor', [(dev, dev ^ hop) for dev in range(4)])]
    ppermute x0 -> x2, waiting for transfers between devices: none -> 1.93 us  [per_device(): lax.ppermute(sketch, 'tensor', [(dev, dev ^ hop) for dev in range(4)])]
    unnamed x8 -> x6, local copies, waits for them, and re-layouts: 1.67 us -> 0.02 us
  transfers between devices with their start and end apart: 1 -> 3, of which waited for: 1 -> 3; matrix products, arithmetic and copies ran while one was open for 0% -> 0% of each run, Pallas kernels for 0% -> 0%
where the time goes in v1:
time: 156 us; the launch traced here: 154 us
  other arithmetic  91.9 us (59%)
  waiting for transfers between devices  21.2 us (14%)
  between operations  16.1 us (10%)
  matrix products  11.4 us (7%)
  local copies, waits for them, and re-layouts  9.49 us (6%)
  starting transfers between devices  4.25 us (3%)
    dynamic_update_slice x14, other arithmetic, per_device(): lax.map(lambda first: projection_block(first, piece_cols, RANK, seeds), s...  82.1 us
    reduce_scatter x1, waiting for transfers between devices, per_device(): lax.psum_scatter(partial_value, 'replica', scatter_dimension=0, tiled=True)  19.3 us
    mul x14, other arithmetic, projection_block(): counter = (column * jnp.int32(rank) + entry) * jnp.int32(2)  9.07 us
    dynamic_slice x14, local copies, waits for them, and re-layouts, per_device(): lax.map(lambda first: projection_block(first, piece_cols, RANK, seeds), s...  8.15 us
    dot_general x1, matrix products, per_device(): lax.dot_general(sketch_rounded, projection, (((1,), (1,)), ((), ())), pre...  6.18 us
    dot_general x1, matrix products, per_device(): jnp.dot(gradient, projection, preferred_element_type=jnp.float32)  5.2 us
    ppermute x2, starting transfers between devices, per_device(): lax.ppermute(sketch, 'tensor', [(dev, dev ^ hop) for dev in range(4)])  4.22 us
  transfers between devices with their start and end apart: 3, of which 3 were waited for; matrix products, arithmetic and copies ran while one was open for 0% of the time, Pallas kernels for 0%

profile of v1, /device:TPU:1, one launch (start us, length us, event | category | flops | bytes accessed | tf_op | source)
XLA Modules:
  0.0 154.5 jit_solution(4229950016771891826)
XLA Ops:
  7.2 1.3 fusion.25
  9.9 99.4 %while.12 = (s32[]{:T(128)}, bf16[14,512,512]{2,1,0:T(8,128)(2,1)}, s32[14]{0:T(128)S(1)}, s32[]{:T(128)}, s32[]{:T(128)}) while((s32[]{:T(128)}, bf16[14,512,512]{2,1,0:T(8,128)(2,1)}, s32[14]{0:T(128)S(1)}, s32[]{:T(128)}, s32[]{:T(128)}) %tuple.33), condition=%wide.region_1.2_spmd, body=%wide.region_0.1_spmd.sunk | while | flops 9176066 | bytes 529485 | solution.py:45
  9.9 0.6 dynamic_slice.8
  10.5 0.6 add_multiply_fusion.2
  11.1 5.9 %fusion.29 = bf16[14,512,512]{2,1,0:T(8,128)(2,1)} fusion(bf16[14,512,512]{2,1,0:T(8,128)(2,1)} %get-tuple-element.105, s32[]{:T(128)} %get-tuple-element.104, s32[]{:T(128)} %get-tuple-element.112, s32[512]{0:T(512)S(1)} %add_multiply_fusion.2), kind=kLoop, calls=%fused_computation.25.clone.1 | loop fusion | flops 9175040 | bytes 527360 | tf_op jit(solution)/shard_map/while/body/jit(dynamic_update_index_in_dim)/dynamic_update_slice | solution.py:45
  17.0 0.6 dynamic_slice.8
  17.6 0.6 add_multiply_fusion.2
  18.2 5.9 %fusion.29 = bf16[14,512,512]{2,1,0:T(8,128)(2,1)} fusion(bf16[14,512,512]{2,1,0:T(8,128)(2,1)} %get-tuple-element.105, s32[]{:T(128)} %get-tuple-element.104, s32[]{:T(128)} %get-tuple-element.112, s32[512]{0:T(512)S(1)} %add_multiply_fusion.2), kind=kLoop, calls=%fused_computation.25.clone.1 | loop fusion | flops 9175040 | bytes 527360 | tf_op jit(solution)/shard_map/while/body/jit(dynamic_update_index_in_dim)/dynamic_update_slice | solution.py:45
  24.1 0.6 dynamic_slice.8
  24.7 0.6 add_multiply_fusion.2
  25.3 5.9 %fusion.29 = bf16[14,512,512]{2,1,0:T(8,128)(2,1)} fusion(bf16[14,512,512]{2,1,0:T(8,128)(2,1)} %get-tuple-element.105, s32[]{:T(128)} %get-tuple-element.104, s32[]{:T(128)} %get-tuple-element.112, s32[512]{0:T(512)S(1)} %add_multiply_fusion.2), kind=kLoop, calls=%fused_computation.25.clone.1 | loop fusion | flops 9175040 | bytes 527360 | tf_op jit(solution)/shard_map/while/body/jit(dynamic_update_index_in_dim)/dynamic_update_slice | solution.py:45
  31.2 0.6 dynamic_slice.8
  31.8 0.6 add_multiply_fusion.2
  32.4 5.9 %fusion.29 = bf16[14,512,512]{2,1,0:T(8,128)(2,1)} fusion(bf16[14,512,512]{2,1,0:T(8,128)(2,1)} %get-tuple-element.105, s32[]{:T(128)} %get-tuple-element.104, s32[]{:T(128)} %get-tuple-element.112, s32[512]{0:T(512)S(1)} %add_multiply_fusion.2), kind=kLoop, calls=%fused_computation.25.clone.1 | loop fusion | flops 9175040 | bytes 527360 | tf_op jit(solution)/shard_map/while/body/jit(dynamic_update_index_in_dim)/dynamic_update_slice | solution.py:45
  38.3 0.6 dynamic_slice.8
  38.9 0.6 add_multiply_fusion.2
  39.5 5.9 %fusion.29 = bf16[14,512,512]{2,1,0:T(8,128)(2,1)} fusion(bf16[14,512,512]{2,1,0:T(8,128)(2,1)} %get-tuple-element.105, s32[]{:T(128)} %get-tuple-element.104, s32[]{:T(128)} %get-tuple-element.112, s32[512]{0:T(512)S(1)} %add_multiply_fusion.2), kind=kLoop, calls=%fused_computation.25.clone.1 | loop fusion | flops 9175040 | bytes 527360 | tf_op jit(solution)/shard_map/while/body/jit(dynamic_update_index_in_dim)/dynamic_update_slice | solution.py:45
  45.4 0.6 dynamic_slice.8
  46.0 0.6 add_multiply_fusion.2
  46.6 5.9 %fusion.29 = bf16[14,512,512]{2,1,0:T(8,128)(2,1)} fusion(bf16[14,512,512]{2,1,0:T(8,128)(2,1)} %get-tuple-element.105, s32[]{:T(128)} %get-tuple-element.104, s32[]{:T(128)} %get-tuple-element.112, s32[512]{0:T(512)S(1)} %add_multiply_fusion.2), kind=kLoop, calls=%fused_computation.25.clone.1 | loop fusion | flops 9175040 | bytes 527360 | tf_op jit(solution)/shard_map/while/body/jit(dynamic_update_index_in_dim)/dynamic_update_slice | solution.py:45
  52.5 0.6 dynamic_slice.8
  53.1 0.6 add_multiply_fusion.2
  53.7 5.9 %fusion.29 = bf16[14,512,512]{2,1,0:T(8,128)(2,1)} fusion(bf16[14,512,512]{2,1,0:T(8,128)(2,1)} %get-tuple-element.105, s32[]{:T(128)} %get-tuple-element.104, s32[]{:T(128)} %get-tuple-element.112, s32[512]{0:T(512)S(1)} %add_multiply_fusion.2), kind=kLoop, calls=%fused_computation.25.clone.1 | loop fusion | flops 9175040 | bytes 527360 | tf_op jit(solution)/shard_map/while/body/jit(dynamic_update_index_in_dim)/dynamic_update_slice | solution.py:45
  59.6 0.6 dynamic_slice.8
  60.2 0.6 add_multiply_fusion.2
  60.8 5.9 %fusion.29 = bf16[14,512,512]{2,1,0:T(8,128)(2,1)} fusion(bf16[14,512,512]{2,1,0:T(8,128)(2,1)} %get-tuple-element.105, s32[]{:T(128)} %get-tuple-element.104, s32[]{:T(128)} %get-tuple-element.112, s32[512]{0:T(512)S(1)} %add_multiply_fusion.2), kind=kLoop, calls=%fused_computation.25.clone.1 | loop fusion | flops 9175040 | bytes 527360 | tf_op jit(solution)/shard_map/while/body/jit(dynamic_update_index_in_dim)/dynamic_update_slice | solution.py:45
  66.7 0.6 dynamic_slice.8
  67.3 0.6 add_multiply_fusion.2
  67.9 5.9 %fusion.29 = bf16[14,512,512]{2,1,0:T(8,128)(2,1)} fusion(bf16[14,512,512]{2,1,0:T(8,128)(2,1)} %get-tuple-element.105, s32[]{:T(128)} %get-tuple-element.104, s32[]{:T(128)} %get-tuple-element.112, s32[512]{0:T(512)S(1)} %add_multiply_fusion.2), kind=kLoop, calls=%fused_computation.25.clone.1 | loop fusion | flops 9175040 | bytes 527360 | tf_op jit(solution)/shard_map/while/body/jit(dynamic_update_index_in_dim)/dynamic_update_slice | solution.py:45
  74.4 0.6 add_multiply_fusion.2
  75.0 5.9 %fusion.29 = bf16[14,512,512]{2,1,0:T(8,128)(2,1)} fusion(bf16[14,512,512]{2,1,0:T(8,128)(2,1)} %get-tuple-element.105, s32[]{:T(128)} %get-tuple-element.104, s32[]{:T(128)} %get-tuple-element.112, s32[512]{0:T(512)S(1)} %add_multiply_fusion.2), kind=kLoop, calls=%fused_computation.25.clone.1 | loop fusion | flops 9175040 | bytes 527360 | tf_op jit(solution)/shard_map/while/body/jit(dynamic_update_index_in_dim)/dynamic_update_slice | solution.py:45
  80.9 0.6 dynamic_slice.8
  81.5 0.6 add_multiply_fusion.2
  82.1 5.9 %fusion.29 = bf16[14,512,512]{2,1,0:T(8,128)(2,1)} fusion(bf16[14,512,512]{2,1,0:T(8,128)(2,1)} %get-tuple-element.105, s32[]{:T(128)} %get-tuple-element.104, s32[]{:T(128)} %get-tuple-element.112, s32[512]{0:T(512)S(1)} %add_multiply_fusion.2), kind=kLoop, calls=%fused_computation.25.clone.1 | loop fusion | flops 9175040 | bytes 527360 | tf_op jit(solution)/shard_map/while/body/jit(dynamic_update_index_in_dim)/dynamic_update_slice | solution.py:45
  88.6 0.6 add_multiply_fusion.2
  89.2 5.9 %fusion.29 = bf16[14,512,512]{2,1,0:T(8,128)(2,1)} fusion(bf16[14,512,512]{2,1,0:T(8,128)(2,1)} %get-tuple-element.105, s32[]{:T(128)} %get-tuple-element.104, s32[]{:T(128)} %get-tuple-element.112, s32[512]{0:T(512)S(1)} %add_multiply_fusion.2), kind=kLoop, calls=%fused_computation.25.clone.1 | loop fusion | flops 9175040 | bytes 527360 | tf_op jit(solution)/shard_map/while/body/jit(dynamic_update_index_in_dim)/dynamic_update_slice | solution.py:45
  95.7 0.6 add_multiply_fusion.2
  96.3 5.9 %fusion.29 = bf16[14,512,512]{2,1,0:T(8,128)(2,1)} fusion(bf16[14,512,512]{2,1,0:T(8,128)(2,1)} %get-tuple-element.105, s32[]{:T(128)} %get-tuple-element.104, s32[]{:T(128)} %get-tuple-element.112, s32[512]{0:T(512)S(1)} %add_multiply_fusion.2), kind=kLoop, calls=%fused_computation.25.clone.1 | loop fusion | flops 9175040 | bytes 527360 | tf_op jit(solution)/shard_map/while/body/jit(dynamic_update_index_in_dim)/dynamic_update_slice | solution.py:45
  102.8 0.6 add_multiply_fusion.2
  103.4 5.9 %fusion.29 = bf16[14,512,512]{2,1,0:T(8,128)(2,1)} fusion(bf16[14,512,512]{2,1,0:T(8,128)(2,1)} %get-tuple-element.105, s32[]{:T(128)} %get-tuple-element.104, s32[]{:T(128)} %get-tuple-element.112, s32[512]{0:T(512)S(1)} %add_multiply_fusion.2), kind=kLoop, calls=%fused_computation.25.clone.1 | loop fusion | flops 9175040 | bytes 527360 | tf_op jit(solution)/shard_map/while/body/jit(dynamic_update_index_in_dim)/dynamic_update_slice | solution.py:45
  109.3 5.2 %fusion.20 = f32[64,512]{1,0:T(8,128)} fusion(bf16[7168,512]{1,0:T(8,128)(2,1)} %bitcast.14, bf16[1,64,7168]{2,1,0:T(8,128)(2,1)S(1)} %copy-done), kind=kOutput, calls=%fused_computation.28 | convolution fusion | flops 469794816 | bytes 8388608 | tf_op jit(solution)/shard_map/dot_general | solution.py:47
  114.5 19.3 %reduce-scatter.2.cloned.1.call-done = f32[16,512]{1,0:T(8,128)} async-done(((f32[64,512]{1,0:T(8,128)}), f32[16,512]{1,0:T(8,128)}) %reduce-scatter.2.cloned.1.call-update) | async-done | bytes 32784 | tf_op jit(solution)/shard_map/reduce_scatter | solution.py:50
  133.8 3.0 %collective-permute-start = (f32[16,512]{1,0:T(8,128)}, f32[16,512]{1,0:T(8,128)S(1)}, u32[]{:S(2)}, u32[]{:S(2)}) collective-permute-start(f32[16,512]{1,0:T(8,128)} %reduce-scatter.2.cloned.1.call-done), channel_id=1, source_target_pairs={{0,8},{8,0},{16,24},{24,16},{1,9},{9,1},{17,25},{25,17},{2,10},{10... | collective-permute-start | bytes 98312 | tf_op jit(solution)/shard_map/ppermute | solution.py:53
  136.9 1.1 collective-permute-done
  137.9 0.8 add.96
  138.7 1.2 collective-permute-start.1
  140.6 0.9 collective-permute-done.1
  141.5 6.2 %multiply_divide_fusion = (f32[16,7168]{1,0:T(8,128)}, f32[16,7168]{1,0:T(8,128)}, f32[16,7168]{1,0:T(8,128)}) fusion(f32[]{:T(128)} %bitcast.6, f32[]{:T(128)} %bitcast.5, f32[16,7168]{1,0:T(8,128)S(1)} %copy-done.1, f32[16,7168]{1,0:T(8,128)S(1)} %copy-done.2, bf16[7168,512]{1,0:T(8,128)(2,1)} %bitcast.15, f32[16,512]{1,0:T(8,128)S(1)} %add.96, ...), kind=kOutput, calls=%fused_computation.32 | convolution fusion | flops 118718464 | bytes 9699336 | tf_op jit(solution)/shard_map/dot_general | solution.py:55
  (14 shorter events, 2.4 us)
Async XLA Ops:
  7.2 102.1 %copy-start = (bf16[1,64,7168]{2,1,0:T(8,128)(2,1)S(1)}, bf16[1,64,7168]{2,1,0:T(8,128)(2,1)}, u32[]{:S(2)}) copy-start(bf16[1,64,7168]{2,1,0:T(8,128)(2,1)} %param.7) | copy-start | bytes 2752516
  7.2 126.6 %reduce-scatter.2.cloned.1.call-start = ((), (), s32[]{:S(2)}) async-start(), calls=%async_computation.1 | async-start | bytes 163840 | tf_op jit(solution)/shard_map/reduce_scatter | solution.py:50
  109.3 32.2 %copy-start.1 = (f32[16,7168]{1,0:T(8,128)S(1)}, f32[16,7168]{1,0:T(8,128)}, u32[]{:S(2)}) copy-start(f32[16,7168]{1,0:T(8,128)} %param.11) | copy-start | bytes 1376260
  109.3 32.2 %copy-start.2 = (f32[16,7168]{1,0:T(8,128)S(1)}, f32[16,7168]{1,0:T(8,128)}, u32[]{:S(2)}) copy-start(f32[16,7168]{1,0:T(8,128)} %param.10) | copy-start | bytes 1376260
  133.8 4.1 %collective-permute-start = (f32[16,512]{1,0:T(8,128)}, f32[16,512]{1,0:T(8,128)S(1)}, u32[]{:S(2)}, u32[]{:S(2)}) collective-permute-start(f32[16,512]{1,0:T(8,128)} %reduce-scatter.2.cloned.1.call-done), channel_id=1, source_target_pairs={{0,8},{8,0},{16,24},{24,16},{1,9},{9,1},{17,25},{25,17},{2,10},{10... | collective-permute-start | bytes 98312 | tf_op jit(solution)/shard_map/ppermute | solution.py:53
  138.7 2.8 %collective-permute-start.1 = (f32[16,512]{1,0:T(8,128)S(1)}, f32[16,512]{1,0:T(8,128)S(1)}, u32[]{:S(2)}, u32[]{:S(2)}) collective-permute-start(f32[16,512]{1,0:T(8,128)S(1)} %add.96), channel_id=1, source_target_pairs={{0,16},{8,24},{16,0},{24,8},{1,17},{9,25},{17,1},{25,9},{2,18},{10... | collective-permute-start | bytes 98312 | tf_op jit(solution)/shard_map/ppermute | solution.py:53
Sparse Core Ops, SparseCore 0:
  114.6 19.1 reduce-scatter.1
